TPU v7x, 512 devices: a whole 4x8x8 slice. The times are simulated.
512 devices in a mesh: seq: 128 (over z, y, core), tp: 4 (over x).
Axes of the slice: x: 4, y: 8, z: 8, core: 2. Of those that a mesh axis runs over, the one named last changes fastest.
Arguments:
- hidden_in: bfloat16 [16384, 1536], P('seq'), may hold values from -6 to 6
- w_query: bfloat16 [1536, 1536], P(None, 'tp'), may hold values from -0.625 to 0.625
- key_weight: bfloat16 [1536, 512], P(None, 'tp'), may hold values from -0.625 to 0.625
- value_weight: bfloat16 [1536, 512], P(None, 'tp'), may hold values from -0.15625 to 0.15625
- w_out: bfloat16 [1536, 1536], P('tp'), may hold values from -0.4375 to 0.4375
- cached_prefix_keys: bfloat16 [4096, 512], P('seq', 'tp'), may hold values from -60000 to 60000
- cached_prefix_values: bfloat16 [4096, 512], P('seq', 'tp'), may hold values from -6 to 6
- doc_ids: int32 [128, 128], P('seq'), may hold values from 0 to 3, never falling along the last dimension, each value on 1 to 64 neighbouring positions
- routes: int32 [16384, 8], P(('seq', 'tp')), may hold values from 0 to 31, all different within a row; in each aligned block of 32 rows (0 to 31, 32 to 63, ...) at most 16 rows name the same one
- gate_scores: float32 [16384, 8], P(('seq', 'tp')), may hold values from 0.2 to 1
- expert_in: bfloat16 [128, 1536, 256], P('seq'), may hold values from -0.15625 to 0.15625
- expert_out: bfloat16 [128, 128, 1536], P('seq'), may hold values from -0.25 to 0.25
Outputs:
- attn_proj: bfloat16 [16384, 1536], P(('seq', 'tp'))
- expert_mix: bfloat16 [16384, 1536], P(('seq', 'tp'))
- layer_out: bfloat16 [16384, 1536], P(('seq', 'tp'))
Inputs may be any that keep to these rules, and one draw needn't show every extreme that they name: `routes`: within the rows of one device (aligned blocks of 32 tokens) no expert is picked by more than 16 tokens, a bound that some block reaches; every expert is picked somewhere.
All inputs are finite; a program needn't handle non-finite values.
Results may differ from a plain program's by a relative error of at most 0.028.
Values may be sent and summed in bfloat16 or wider, within the bound.
No kernel may reach another device: no remote copies, remote signals or barrier semaphores. Data moves between devices by JAX's collectives and lax.ppermute only.
A program may use at most 64 MiB of HBM per device.

v0:
```python
import jax
import jax.numpy as jnp
from jax import lax
from jax.sharding import PartitionSpec as P

HEAD_WIDTH = 64
EXPERTS = 32
EPSILON = 1e-06
RESIDUAL = 0.22


def normalize(values):
    values = values.astype(jnp.float32)
    return values * lax.rsqrt(jnp.mean(values * values, axis=-1, keepdims=True) + EPSILON)


def rotary_apply(values, token_positions):
    half_size = values.shape[-1] // 2
    frequency = jnp.exp(
        -jnp.log(10000.0) * jnp.arange(half_size, dtype=jnp.float32) * 2.0 / values.shape[-1]
    )
    angles = token_positions[:, None] * frequency[None, :]
    cosine = jnp.cos(angles)[:, None, :]
    sine_part = jnp.sin(angles)[:, None, :]
    first_half = values[..., :half_size]
    second = values[..., half_size:]
    return jnp.concatenate(
        [first_half * cosine - second * sine_part, second * cosine + first_half * sine_part],
        axis=-1,
    )


def body(
    hidden_in,
    w_query,
    key_weight,
    value_weight,
    w_out,
    cached_prefix_keys,
    cached_prefix_values,
    doc_ids,
    routes,
    gate_scores,
    expert_in,
    expert_out,
):
    rows_dev = hidden_in.shape[0]
    column_list = hidden_in.shape[1]
    head_size = HEAD_WIDTH
    kv_local = key_weight.shape[1] // head_size
    group_width = w_query.shape[1] // head_size // kv_local
    seq_count = lax.axis_size("seq")
    prefix_len = cached_prefix_keys.shape[0] * seq_count
    doc_row = doc_ids[0]
    row_index = jnp.arange(rows_dev, dtype=jnp.int32)
    same_doc = doc_row[:, None] == doc_row[None, :]
    doc_start = jnp.min(jnp.where(same_doc, row_index[None, :], rows_dev), axis=1)
    token_positions = (prefix_len + row_index - doc_start).astype(jnp.float32)
    normed_input = normalize(hidden_in).astype(jnp.bfloat16)
    query_rows_all = jnp.dot(normed_input, w_query, preferred_element_type=jnp.float32).reshape(
        rows_dev, kv_local * group_width, head_size
    )
    query_rows_all = (
        rotary_apply(query_rows_all, token_positions)
        .astype(jnp.bfloat16)
        .reshape(rows_dev, kv_local, group_width, head_size)
    )
    fresh_key = jnp.dot(normed_input, key_weight, preferred_element_type=jnp.float32).reshape(
        rows_dev, kv_local, head_size
    )
    fresh_key = rotary_apply(fresh_key, token_positions).astype(jnp.bfloat16)
    fresh_value = (
        jnp.dot(normed_input, value_weight, preferred_element_type=jnp.float32)
        .astype(jnp.bfloat16)
        .reshape(rows_dev, kv_local, head_size)
    )
    own_scores = (
        jnp.einsum("tkgd,skd->tkgs", query_rows_all, fresh_key, preferred_element_type=jnp.float32)
        / head_size
    )
    visible = same_doc & (row_index[None, :] <= row_index[:, None])
    own_scores = jnp.where(visible[:, None, None, :], own_scores, -jnp.inf)
    row_top = jnp.max(own_scores, axis=-1)
    weights = jnp.exp(own_scores - row_top[..., None])
    denominator = jnp.sum(weights, axis=-1)
    numerator = jnp.einsum(
        "tkgs,skd->tkgd",
        weights.astype(jnp.bfloat16),
        fresh_value,
        preferred_element_type=jnp.float32,
    )
    running = (row_top, denominator, numerator)
    whole_keys, whole_values = (
        lax.all_gather(cached_prefix_keys, "seq", axis=0, tiled=True),
        lax.all_gather(cached_prefix_values, "seq", axis=0, tiled=True),
    )
    top_old, denom_old, numer_old = running
    key_rows = whole_keys.reshape(-1, kv_local, head_size)
    value_rows = whole_values.reshape(-1, kv_local, head_size)
    scores = (
        jnp.einsum("tkgd,pkd->tkgp", query_rows_all, key_rows, preferred_element_type=jnp.float32)
        / head_size
    )
    top_new = jnp.maximum(top_old, jnp.max(scores, axis=-1))
    shrink = jnp.exp(top_old - top_new)
    part_weights = jnp.exp(scores - top_new[..., None])
    denom_new = denom_old * shrink + jnp.sum(part_weights, axis=-1)
    numer_new = numer_old * shrink[..., None] + jnp.einsum(
        "tkgp,pkd->tkgd",
        part_weights.astype(jnp.bfloat16),
        value_rows,
        preferred_element_type=jnp.float32,
    )
    running = (top_new, denom_new, numer_new)
    attended = (
        (running[2] / running[1][..., None])
        .astype(jnp.bfloat16)
        .reshape(rows_dev, kv_local * group_width * head_size)
    )
    moe_rows = routes.shape[0]
    row_start = lax.axis_index("tp") * moe_rows
    summed_all = lax.psum(jnp.dot(attended, w_out, preferred_element_type=jnp.float32), "tp")
    attn_sum = lax.dynamic_slice_in_dim(summed_all, row_start, moe_rows, 0)
    residual = (
        lax.dynamic_slice_in_dim(hidden_in, row_start, moe_rows, 0).astype(jnp.float32)
        + RESIDUAL * attn_sum
    )
    routed = normalize(residual).astype(jnp.bfloat16)
    experts = EXPERTS
    units_dev = expert_in.shape[0]
    hparts = units_dev * seq_count // experts
    capacity = moe_rows // 2
    ff_part = expert_out.shape[1]
    onehot = (routes[:, :, None] == jnp.arange(experts, dtype=jnp.int32)[None, None, :]).astype(
        jnp.int32
    )
    per_row = jnp.sum(onehot, axis=1)
    before = jnp.cumsum(per_row, axis=0) - per_row
    rank_in = jnp.sum(onehot * before[:, None, :], axis=2)
    slot_of = routes * capacity + rank_in
    slot_ids = jnp.arange(experts * capacity, dtype=jnp.int32)
    pick_hit = slot_of[:, :, None] == slot_ids[None, None, :]
    selector = jnp.any(pick_hit, axis=1).T.astype(jnp.bfloat16)
    combiner = jnp.sum(jnp.where(pick_hit, gate_scores[:, :, None], 0.0), axis=1)
    gathered = jnp.dot(selector, routed, preferred_element_type=jnp.float32).astype(jnp.bfloat16)
    outgoing = jnp.broadcast_to(
        gathered.reshape(experts, 1, capacity, column_list),
        (experts, hparts, capacity, column_list),
    )
    outgoing = outgoing.reshape(seq_count, units_dev, capacity, column_list)
    gate_up = jnp.einsum(
        "sucd,udf->sucf",
        lax.all_to_all(outgoing, "seq", split_axis=0, concat_axis=0, tiled=True),
        expert_in,
        preferred_element_type=jnp.float32,
    )
    activated = (jax.nn.silu(gate_up[..., :ff_part]) * gate_up[..., ff_part:]).astype(jnp.bfloat16)
    partial_value = jnp.einsum(
        "sucf,ufd->sucd", activated, expert_out, preferred_element_type=jnp.float32
    ).astype(jnp.bfloat16)
    returned = lax.all_to_all(partial_value, "seq", split_axis=0, concat_axis=0, tiled=True)
    part_sum = jnp.sum(
        returned.reshape(experts, hparts, capacity, column_list).astype(jnp.float32), axis=1
    )
    part_sum = part_sum.reshape(experts * capacity, column_list)
    expert_sum = jnp.dot(
        combiner, part_sum, precision=lax.Precision.HIGHEST, preferred_element_type=jnp.float32
    )
    layer_out = (residual + RESIDUAL * expert_sum).astype(jnp.bfloat16)
    return (attn_sum.astype(jnp.bfloat16), expert_sum.astype(jnp.bfloat16), layer_out)


def solution(mesh):
    in_specs = (
        P("seq", None),
        P(None, "tp"),
        P(None, "tp"),
        P(None, "tp"),
        P("tp", None),
        P("seq", "tp"),
        P("seq", "tp"),
        P("seq", None),
        P(("seq", "tp"), None),
        P(("seq", "tp"), None),
        P("seq", None, None),
        P("seq", None, None),
    )
    out_specs = (P(("seq", "tp"), None), P(("seq", "tp"), None), P(("seq", "tp"), None))
    return jax.shard_map(body, mesh=mesh, in_specs=in_specs, out_specs=out_specs, check_vma=False)
```

profile of v0, /device:TPU:17, one launch (start us, length us, event | category | flops | bytes accessed | tf_op | source)
XLA Modules:
  0.0 620.2 jit_solution(3944682123108635875)
XLA Ops:
  7.2 0.7 all-gather.3.cloned.1.call-update
  8.0 0.7 all-gather.5.cloned.1.call-update
  8.7 1.2 fusion.21
  9.9 0.8 fusion.33
  10.7 2.0 fusion.43
  12.7 1.5 fusion.45
  14.4 0.8 compare_and_fusion
  15.2 0.3 fusion.48
  15.6 1.5 convolution_convert_fusion.1
  17.1 77.1 %all-gather.3.cloned.1.call-done = bf16[4096,128]{1,0:T(8,128)(2,1)} async-done(((bf16[32,128]{1,0:T(8,128)(2,1)}), bf16[4096,128]{1,0:T(8,128)(2,1)}) %all-gather.3.cloned.1.call-update) | async-done | bytes 1048592 | tf_op jit(solution)/shard_map/all_gather | solution.py:94
  94.2 1.5 copy.68
  95.7 1.9 bitcast_reduce_fusion
  97.6 4.6 copy-done.1
  102.2 2.2 fusion.1
  104.3 67.8 %all-gather.5.cloned.1.call-done = bf16[4096,128]{1,0:T(8,128)(2,1)} async-done(((bf16[32,128]{1,0:T(8,128)(2,1)}), bf16[4096,128]{1,0:T(8,128)(2,1)}) %all-gather.5.cloned.1.call-update) | async-done | bytes 1048592 | tf_op jit(solution)/shard_map/all_gather | solution.py:95
  172.1 1.5 copy.69
  173.7 5.9 fusion.16
  179.8 1.3 fusion.49
  181.4 0.7 select_reduce_fusion.1
  182.5 48.2 %all-reduce.2.cloned.1.call-done = f32[128,1536]{1,0:T(8,128)} async-done(((f32[128,1536]{1,0:T(8,128)}), f32[128,1536]{1,0:T(8,128)}) %all-reduce.2.cloned.1.call-update) | async-done | bytes 786448 | tf_op jit(solution)/shard_map/psum | solution.py:122
  230.7 1.1 multiply_reduce_fusion
  231.7 1.6 convolution_convert_fusion
  233.3 0.8 broadcast_in_dim.40
  234.1 158.0 %all_to_all.10 = bf16[128,1,16,1536]{3,2,1,0:T(8,128)(2,1)S(1)} all-to-all(bf16[128,1,16,1536]{3,2,1,0:T(8,128)(2,1)S(1)} %bitcast.102), channel_id=1, replica_groups=mesh['seq'=128,'tp'=4] {'seq'}, dimensions={0} | all-to-all | bytes 12582912 | tf_op jit(solution)/shard_map/all_to_all | solution.py:153
  392.1 7.3 %fusion.8 = f32[128,1,16,256]{3,0,2,1:T(8,128)S(1)} fusion(bf16[128,1,16,1536]{3,2,1,0:T(8,128)(2,1)S(1)} %all_to_all.10, bf16[1,1536,256]{2,1,0:T(8,128)(2,1)S(1)} %copy-done.6), kind=kOutput, calls=%fused_computation.12 | convolution fusion | flops 1610612736 | bytes 9175040 | tf_op jit(solution)/shard_map/sucd,udf->sucf/dot_general | solution.py:151
  399.4 1.8 convert_bitcast_fusion
  401.2 6.4 %copy.75 = bf16[128,1,16,1536]{3,2,1,0:T(8,128)(2,1)} copy(bf16[128,1,16,1536]{3,0,2,1:T(8,128)(2,1)S(1)} %convert_bitcast_fusion) | data formatting | bytes 12582912 | tf_op jit(solution)/shard_map/convert_element_type | solution.py:160
  407.6 21.8 %all-to-all-start.1 = ((bf16[128,1,16,1536]{3,2,1,0:T(8,128)(2,1)}), bf16[128,1,16,1536]{3,2,1,0:T(8,128)(2,1)}, u32[]{:S(2)}, u32[]{:S(2)}) async-start(bf16[128,1,16,1536]{3,2,1,0:T(8,128)(2,1)} %copy.75), calls=%async_computation.1 | async-start | bytes 12582912 | tf_op jit(solution)/shard_map/all_to_all | solution.py:161
  429.7 1.6 dynamic-slice_convert_fusion
  431.3 174.6 %all-to-all-done.1 = bf16[128,1,16,1536]{3,2,1,0:T(8,128)(2,1)} async-done(((bf16[128,1,16,1536]{3,2,1,0:T(8,128)(2,1)}), bf16[128,1,16,1536]{3,2,1,0:T(8,128)(2,1)}, u32[]{:S(2)}, u32[]{:S(2)}) %all-to-all-start.1) | async-done | bytes 6291488 | tf_op jit(solution)/shard_map/all_to_all | solution.py:161
  605.9 4.3 convert_reduce_fusion
  610.2 3.5 add_convert_fusion
  (38 shorter events, 1.6 us)
Async XLA Ops:
  7.2 172.6 %copy-start = (bf16[384,1536]{1,0:T(8,128)(2,1)S(1)}, bf16[384,1536]{1,0:T(8,128)(2,1)}, u32[]{:S(2)}) copy-start(bf16[384,1536]{1,0:T(8,128)(2,1)} %param.16) | copy-start | bytes 3538948
  7.2 87.0 %all-gather.3.cloned.1.call-start = ((), (), s32[]{:S(2)}) async-start(), calls=%async_computation.2 | async-start | bytes 1056768 | tf_op jit(solution)/shard_map/all_gather | solution.py:94
  7.9 164.2 %all-gather.5.cloned.1.call-start = ((), (), s32[]{:S(2)}) async-start(), calls=%async_computation.3 | async-start | bytes 1056768 | tf_op jit(solution)/shard_map/all_gather | solution.py:95
  8.7 222.0 %all-reduce.2.cloned.1.call-start = ((), (), s32[]{:S(2)}) async-start(), calls=%async_computation.4 | async-start | bytes 1572864 | tf_op jit(solution)/shard_map/psum | solution.py:122
  97.6 4.6 copy-start.1
  173.6 7.5 %copy-start.4 = (s32[32,8]{0,1:T(8,128)S(1)}, s32[32,8]{0,1:T(8,128)}, u32[]{:S(2)}) copy-start(s32[32,8]{0,1:T(8,128)} %param.20) | copy-start | bytes 3076
  173.6 57.0 %copy-start.2 = (bf16[128,1536]{1,0:T(8,128)(2,1)S(1)}, bf16[128,1536]{1,0:T(8,128)(2,1)}, u32[]{:S(2)}) copy-start(bf16[128,1536]{1,0:T(8,128)(2,1)} %param.12) | copy-start | bytes 1179652
  234.1 158.0 %copy-start.6 = (bf16[1,1536,256]{2,1,0:T(8,128)(2,1)S(1)}, bf16[1,1536,256]{2,1,0:T(8,128)(2,1)}, u32[]{:S(2)}) copy-start(bf16[1,1536,256]{2,1,0:T(8,128)(2,1)} %param.22) | copy-start | bytes 2359300
  392.1 7.3 %copy-start.3 = (bf16[1,128,1536]{2,1,0:T(8,128)(2,1)S(1)}, bf16[1,128,1536]{2,1,0:T(8,128)(2,1)}, u32[]{:S(2)}) copy-start(bf16[1,128,1536]{2,1,0:T(8,128)(2,1)} %param.23) | copy-start | bytes 1179652
  407.6 21.8 %copy-start.5 = (f32[32,8]{0,1:T(8,128)S(1)}, f32[32,8]{0,1:T(8,128)}, u32[]{:S(2)}) copy-start(f32[32,8]{0,1:T(8,128)} %param.21) | copy-start | bytes 3076
  407.6 198.3 %all-to-all-start.1 = ((bf16[128,1,16,1536]{3,2,1,0:T(8,128)(2,1)}), bf16[128,1,16,1536]{3,2,1,0:T(8,128)(2,1)}, u32[]{:S(2)}, u32[]{:S(2)}) async-start(bf16[128,1,16,1536]{3,2,1,0:T(8,128)(2,1)} %copy.75), calls=%async_computation.1 | async-start | bytes 12582912 | tf_op jit(solution)/shard_map/all_to_all | solution.py:161
Sparse Core Ops, SparseCore 0:
  11.0 83.1 all-gather.2
  97.2 74.8 all-gather.4
  181.2 49.3 all-reduce.1
where the time goes:
time: 621 us; the launch traced here: 620 us
  waiting for transfers between devices  369 us (59%)
  blocking collectives  158 us (25%)
  matrix products  28.7 us (5%)
  starting transfers between devices  21.9 us (4%)
  local copies, waits for them, and re-layouts  16.6 us (3%)
  between operations  14 us (2%)
  other arithmetic  11.9 us (2%)
    all_to_all x1, waiting for transfers between devices, body(): lax.all_to_all(partial_value, 'seq', split_axis=0, concat_axis=0, tiled=T...  175 us
    all_to_all x1, blocking collectives, body(): lax.all_to_all(outgoing, 'seq', split_axis=0, concat_axis=0, tiled=True)  158 us
    all_gather x1, waiting for transfers between devices, body(): lax.all_gather(cached_prefix_keys, 'seq', axis=0, tiled=True)  77.1 us
    all_gather x1, waiting for transfers between devices, body(): lax.all_gather(cached_prefix_values, 'seq', axis=0, tiled=True)  67.8 us
    psum x1, waiting for transfers between devices, body(): lax.psum(jnp.dot(attended, w_out, preferred_element_type=jnp.float32), 'tp')  48.2 us
    all_to_all x1, starting transfers between devices, body(): lax.all_to_all(partial_value, 'seq', split_axis=0, concat_axis=0, tiled=T...  21.8 us
  transfers between devices with their start and end apart: 4, of which 4 were waited for; matrix products, arithmetic and copies ran while one was open for 3% of the time, Pallas kernels for 0%

commit v1 on v0

--- a/solution.py
+++ b/solution.py
@@ -92,7 +92,10 @@
     running = (row_top, denominator, numerator)
     whole_keys, whole_values = (
         lax.all_gather(cached_prefix_keys, "seq", axis=0, tiled=True),
-        lax.all_gather(cached_prefix_values, "seq", axis=0, tiled=True),
+        jnp.concatenate(
+            lax.all_to_all(jnp.stack([cached_prefix_values] * lax.axis_size("seq")), "seq", 0, 0),
+            axis=0,
+        ),
     )
     top_old, denom_old, numer_old = running
     key_rows = whole_keys.reshape(-1, kv_local, head_size)

time: 621 us -> 574 us (0.924)
  waiting for transfers between devices: 369 us -> 300 us
  starting transfers between devices: 21.9 us -> 39.6 us
    all_gather x1 -> x0, waiting for transfers between devices: 67.8 us -> none  [body(): lax.all_gather(cached_prefix_values, 'seq', axis=0, tiled=True)]
    all_to_all x0 -> x1, starting transfers between devices: none -> 17.5 us  [body(): lax.all_to_all(jnp.stack([cached_prefix_values] * lax.axis_size('seq')),...]
  transfers between devices with their start and end apart: 4 -> 4, of which waited for: 4 -> 3; matrix products, arithmetic and copies ran while one was open for 3% -> 3% of each run, Pallas kernels for 0% -> 0%
where the time goes in v1:
time: 574 us
  waiting for transfers between devices  300 us (52%)
  blocking collectives  158 us (28%)
  starting transfers between devices  39.6 us (7%)
  matrix products  30.5 us (5%)
  local copies, waits for them, and re-layouts  19.8 us (3%)
  between operations  14.3 us (2%)
  other arithmetic  11.2 us (2%)
    all_to_all x1, waiting for transfers between devices, body(): lax.all_to_all(partial_value, 'seq', split_axis=0, concat_axis=0, tiled=T...  175 us
    all_to_all x1, blocking collectives, body(): lax.all_to_all(outgoing, 'seq', split_axis=0, concat_axis=0, tiled=True)  158 us
    all_gather x1, waiting for transfers between devices, body(): lax.all_gather(cached_prefix_keys, 'seq', axis=0, tiled=True)  76.7 us
    psum x1, waiting for transfers between devices, body(): lax.psum(jnp.dot(attended, w_out, preferred_element_type=jnp.float32), 'tp')  48.2 us
    all_to_all x1, starting transfers between devices, body(): lax.all_to_all(partial_value, 'seq', split_axis=0, concat_axis=0, tiled=T...  21.8 us
    all_to_all x1, starting transfers between devices, body(): lax.all_to_all(jnp.stack([cached_prefix_values] * lax.axis_size('seq')),...  17.5 us
  transfers between devices with their start and end apart: 4, of which 3 were waited for; matrix products, arithmetic and copies ran while one was open for 3% of the time, Pallas kernels for 0%

profile of v1, /device:TPU:17, one launch (start us, length us, event | category | flops | bytes accessed | tf_op | source)
XLA Modules:
  0.0 573.6 jit_solution(717489062222583115)
XLA Ops:
  7.2 2.0 stack.2
  9.2 17.5 %all-to-all-start = ((bf16[128,32,128]{2,1,0:T(8,128)(2,1)}), bf16[128,32,128]{2,1,0:T(8,128)(2,1)S(1)}, u32[]{:S(2)}, u32[]{:S(2)}) async-start(bf16[128,32,128]{2,1,0:T(8,128)(2,1)} %stack.2), calls=%async_computation | async-start | bytes 2097152 | tf_op jit(solution)/shard_map/all_to_all | solution.py:96
  26.8 0.7 all-gather.2.cloned.1.call-update
  27.7 1.2 fusion.26
  28.9 0.8 fusion.38
  29.9 1.5 fusion.50
  31.4 2.0 fusion.48
  33.6 0.3 fusion.53
  33.9 0.3 convolution_convert_fusion.1
  34.3 76.7 %all-gather.2.cloned.1.call-done = bf16[4096,128]{1,0:T(8,128)(2,1)} async-done(((bf16[32,128]{1,0:T(8,128)(2,1)}), bf16[4096,128]{1,0:T(8,128)(2,1)}) %all-gather.2.cloned.1.call-update) | async-done | bytes 1048592 | tf_op jit(solution)/shard_map/all_gather | solution.py:94
  111.0 2.3 copy.68
  113.3 3.1 bitcast_reduce_fusion
  116.5 4.6 copy-done.1
  121.0 2.2 fusion.1
  123.2 1.8 reshape_reshape.3
  125.0 7.6 %fusion.19 = f32[128,2,3,64]{0,3,2,1:T(8,128)S(1)} fusion(bf16[4096,2,64,1]{2,1,0,3:T(2,128)(2,1)} %bitcast.99, f32[2,128,3,4096]{3,1,2,0:T(8,128)} %copy-done.1, f32[128,2,3]{0,2,1:T(4,128)S(1)} %max.13), kind=kOutput, calls=%fused_computation.23 | convolution fusion | flops 412090368 | bytes 13831168 | tf_op jit(solution)/shard_map/tkgp,pkd->tkgd/dot_general | solution.py:111
  132.9 1.3 fusion.54
  134.5 0.7 select_reduce_fusion.1
  135.3 0.2 fusion.31
  135.6 48.2 %all-reduce.2.cloned.1.call-done = f32[128,1536]{1,0:T(8,128)} async-done(((f32[128,1536]{1,0:T(8,128)}), f32[128,1536]{1,0:T(8,128)}) %all-reduce.2.cloned.1.call-update) | async-done | bytes 786448 | tf_op jit(solution)/shard_map/psum | solution.py:125
  183.8 1.1 multiply_reduce_fusion
  184.9 1.6 convolution_convert_fusion
  186.5 0.8 broadcast_in_dim.40
  187.3 158.0 %all_to_all.15 = bf16[128,1,16,1536]{3,2,1,0:T(8,128)(2,1)S(1)} all-to-all(bf16[128,1,16,1536]{3,2,1,0:T(8,128)(2,1)S(1)} %bitcast.97), channel_id=1, replica_groups=mesh['seq'=128,'tp'=4] {'seq'}, dimensions={0} | all-to-all | bytes 12582912 | tf_op jit(solution)/shard_map/all_to_all | solution.py:156
  345.3 7.3 %fusion.11 = f32[128,1,16,256]{3,0,2,1:T(8,128)S(1)} fusion(bf16[128,1,16,1536]{3,2,1,0:T(8,128)(2,1)S(1)} %all_to_all.15, bf16[1,1536,256]{2,1,0:T(8,128)(2,1)S(1)} %copy-done.8), kind=kOutput, calls=%fused_computation.15 | convolution fusion | flops 1610612736 | bytes 9175040 | tf_op jit(solution)/shard_map/sucd,udf->sucf/dot_general | solution.py:154
  352.5 1.8 convert_bitcast_fusion
  354.3 6.4 %copy.75 = bf16[128,1,16,1536]{3,2,1,0:T(8,128)(2,1)} copy(bf16[128,1,16,1536]{3,0,2,1:T(8,128)(2,1)S(1)} %convert_bitcast_fusion) | data formatting | bytes 12582912 | tf_op jit(solution)/shard_map/convert_element_type | solution.py:163
  360.7 21.8 %all-to-all-start.2 = ((bf16[128,1,16,1536]{3,2,1,0:T(8,128)(2,1)}), bf16[128,1,16,1536]{3,2,1,0:T(8,128)(2,1)}, u32[]{:S(2)}, u32[]{:S(2)}) async-start(bf16[128,1,16,1536]{3,2,1,0:T(8,128)(2,1)} %copy.75), calls=%async_computation.2 | async-start | bytes 12582912 | tf_op jit(solution)/shard_map/all_to_all | solution.py:164
  382.8 1.6 dynamic-slice_convert_fusion
  384.4 174.6 %all-to-all-done.2 = bf16[128,1,16,1536]{3,2,1,0:T(8,128)(2,1)} async-done(((bf16[128,1,16,1536]{3,2,1,0:T(8,128)(2,1)}), bf16[128,1,16,1536]{3,2,1,0:T(8,128)(2,1)}, u32[]{:S(2)}, u32[]{:S(2)}) %all-to-all-start.2) | async-done | bytes 6291488 | tf_op jit(solution)/shard_map/all_to_all | solution.py:164
  559.0 4.3 convert_reduce_fusion
  563.3 3.5 add_convert_fusion
  (42 shorter events, 1.6 us)
Async XLA Ops:
  7.2 125.7 %copy-start = (bf16[384,1536]{1,0:T(8,128)(2,1)S(1)}, bf16[384,1536]{1,0:T(8,128)(2,1)}, u32[]{:S(2)}) copy-start(bf16[384,1536]{1,0:T(8,128)(2,1)} %param.16) | copy-start | bytes 3538948
  7.2 26.7 %copy-start.2 = (bf16[128,1536]{1,0:T(8,128)(2,1)S(1)}, bf16[128,1536]{1,0:T(8,128)(2,1)}, u32[]{:S(2)}) copy-start(bf16[128,1536]{1,0:T(8,128)(2,1)} %param.12) | copy-start | bytes 1179652
  7.2 26.3 %copy-start.7 = (s32[1,128]{1,0:T(1,128)S(1)}, s32[1,128]{1,0:T(1,128)}, u32[]{:S(2)}) copy-start(s32[1,128]{1,0:T(1,128)} %param.19) | copy-start | bytes 1540
  7.2 26.7 %copy-start.3 = (bf16[1536,128]{1,0:T(8,128)(2,1)S(1)}, bf16[1536,128]{1,0:T(8,128)(2,1)}, u32[]{:S(2)}) copy-start(bf16[1536,128]{1,0:T(8,128)(2,1)} %param.15) | copy-start | bytes 1179652
  9.2 114.0 %all-to-all-start = ((bf16[128,32,128]{2,1,0:T(8,128)(2,1)}), bf16[128,32,128]{2,1,0:T(8,128)(2,1)S(1)}, u32[]{:S(2)}, u32[]{:S(2)}) async-start(bf16[128,32,128]{2,1,0:T(8,128)(2,1)} %stack.2), calls=%async_computation | async-start | bytes 2097152 | tf_op jit(solution)/shard_map/all_to_all | solution.py:96
  26.8 84.2 %all-gather.2.cloned.1.call-start = ((), (), s32[]{:S(2)}) async-start(), calls=%async_computation.3 | async-start | bytes 1056768 | tf_op jit(solution)/shard_map/all_gather | solution.py:94
  27.5 156.3 %all-reduce.2.cloned.1.call-start = ((), (), s32[]{:S(2)}) async-start(), calls=%async_computation.4 | async-start | bytes 1572864 | tf_op jit(solution)/shard_map/psum | solution.py:125
  116.4 4.6 copy-start.1
  125.0 9.2 %copy-start.5 = (s32[32,8]{0,1:T(8,128)S(1)}, s32[32,8]{0,1:T(8,128)}, u32[]{:S(2)}) copy-start(s32[32,8]{0,1:T(8,128)} %param.20) | copy-start | bytes 3076
  187.3 158.0 %copy-start.8 = (bf16[1,1536,256]{2,1,0:T(8,128)(2,1)S(1)}, bf16[1,1536,256]{2,1,0:T(8,128)(2,1)}, u32[]{:S(2)}) copy-start(bf16[1,1536,256]{2,1,0:T(8,128)(2,1)} %param.22) | copy-start | bytes 2359300
  345.3 7.3 %copy-start.4 = (bf16[1,128,1536]{2,1,0:T(8,128)(2,1)S(1)}, bf16[1,128,1536]{2,1,0:T(8,128)(2,1)}, u32[]{:S(2)}) copy-start(bf16[1,128,1536]{2,1,0:T(8,128)(2,1)} %param.23) | copy-start | bytes 1179652
  360.7 21.8 %copy-start.6 = (f32[32,8]{0,1:T(8,128)S(1)}, f32[32,8]{0,1:T(8,128)}, u32[]{:S(2)}) copy-start(f32[32,8]{0,1:T(8,128)} %param.21) | copy-start | bytes 3076
  360.7 198.3 %all-to-all-start.2 = ((bf16[128,1,16,1536]{3,2,1,0:T(8,128)(2,1)}), bf16[128,1,16,1536]{3,2,1,0:T(8,128)(2,1)}, u32[]{:S(2)}, u32[]{:S(2)}) async-start(bf16[128,1,16,1536]{3,2,1,0:T(8,128)(2,1)} %copy.75), calls=%async_computation.2 | async-start | bytes 12582912 | tf_op jit(solution)/shard_map/all_to_all | solution.py:164
Sparse Core Ops, SparseCore 0:
  30.6 80.3 all-gather.1
  134.3 49.4 all-reduce.1
